TPU v7x, 128 devices: a whole 4x4x4 slice. The times are simulated.
128 devices in a mesh: blk: 8 (over y_lo, x), dp: 16 (over z, y_hi, core).
Axes of the slice: x: 4, y: 4 (y_hi: 2, y_lo: 2; y = y_hi * 2 + y_lo), z: 4, core: 2. Of those that a mesh axis runs over, the one named last changes fastest.
Arguments:
- train_grads: bfloat16 [8192, 8192], P(('blk', 'dp')), may hold values from -6 to 6
- train_scale: bfloat16 [8192], P(('blk', 'dp')), may hold values from 0.5 to 4
- train_class: int32 [8192], P(('blk', 'dp')), may hold values from 0 to 511
- test_grads: bfloat16 [8192, 8192], P(('blk', 'dp')), may hold values from -0.099609375 to 0.099609375
- test_class: int32 [8192], P(('blk', 'dp')), may hold values from 0 to 511
Outputs:
- train_attr: float32 [8192, 512], P(('blk', 'dp'))
- test_attr: float32 [8192], P(('blk', 'dp'))
All inputs are finite; a program needn't handle non-finite values.
Results may differ from a plain program's by a relative error of at most 0.0021.
Values may be sent and summed in bfloat16 or wider, within the bound.
No kernel may reach another device: no remote copies, remote signals or barrier semaphores. Data moves between devices by JAX's collectives and lax.ppermute only.
A program may use at most 128 MiB of HBM per device.

v0:
```python
import jax
import jax.numpy as jnp
from jax import lax
from jax.sharding import PartitionSpec as P

NCLS = 512
PAD = 128


def indicator(labels):
    columns = lax.broadcasted_iota(jnp.int32, (labels.shape[0], NCLS), 1)
    return (labels[:, None] == columns).astype(jnp.bfloat16)


def with_side(grads, side, first):
    rows = grads.shape[0]
    cols = lax.broadcasted_iota(jnp.int32, (rows, PAD), 1)
    extra = jnp.zeros((rows, PAD), jnp.bfloat16)
    for k, v in enumerate(side):
        extra = jnp.where(cols == first + k, v[:, None].astype(jnp.bfloat16), extra)
    return jnp.concatenate([grads, extra], axis=1)


def split_class(c):
    return (c // 32, c % 32)


def join_class(x, k):
    hi = x[:, k].astype(jnp.int32)
    lo = x[:, k + 1].astype(jnp.int32)
    return hi * 32 + lo


def local(train_grads, train_scale, train_class, test_grads, test_class):
    k = train_grads.shape[1]
    tr = with_side(train_grads, (train_scale,) + split_class(train_class), 0)
    te = with_side(test_grads, split_class(test_class), 4)
    tr_all = lax.all_gather(tr, "blk", axis=0, tiled=True)
    te_all = lax.all_gather(te, "dp", axis=0, tiled=True)
    raw = lax.dot_general(
        tr_all, te_all, (((1,), (1,)), ((), ())), preferred_element_type=jnp.float32
    )
    scale = tr_all[:, k].astype(jnp.float32)
    weights = jnp.tanh(scale[:, None] * raw).astype(jnp.bfloat16)
    train_hot = indicator(join_class(tr_all, k + 1))
    test_hot = indicator(join_class(te_all, k + 4))
    part = jnp.dot(weights, test_hot, preferred_element_type=jnp.float32)
    per_class = lax.dot_general(
        weights, train_hot, (((0,), (0,)), ((), ())), preferred_element_type=jnp.float32
    )
    test_part = jnp.sum(per_class * test_hot.astype(jnp.float32), axis=1)
    train_attr = lax.psum_scatter(part, "blk", scatter_dimension=0, tiled=True)
    test_attr = lax.psum_scatter(test_part, "dp", scatter_dimension=0, tiled=True)
    return (train_attr, test_attr)


def solution(mesh):
    in_specs = (
        P(("blk", "dp"), None),
        P(("blk", "dp")),
        P(("blk", "dp")),
        P(("blk", "dp"), None),
        P(("blk", "dp")),
    )
    out_specs = (P(("blk", "dp"), None), P(("blk", "dp")))
    return jax.shard_map(local, mesh=mesh, in_specs=in_specs, out_specs=out_specs, check_vma=False)
```

profile of v0, /device:TPU:6, one launch (start us, length us, event | category | flops | bytes accessed | tf_op | source)
XLA Modules:
  0.0 282.2 jit_solution(7258270787479759474)
XLA Ops:
  7.2 0.0 all-gather.3.cloned.1.call-start
  7.3 0.7 fusion.4
  8.0 0.7 select_select_fusion.1
  8.7 2.3 pad_maximum_fusion
  11.1 0.0 all-gather.3.cloned.1.call-update
  11.1 0.0 all-gather.5.cloned.1.call-start
  11.2 0.1 select_select_fusion
  11.3 0.0 copy-done
  11.3 1.1 pad_maximum_fusion.1
  12.4 0.0 all-gather.5.cloned.1.call-update
  12.4 0.0 reduce-scatter.2.cloned.1.call-start
  12.4 92.1 %all-gather.3.cloned.1.call-done = bf16[512,8320]{1,0:T(8,128)(2,1)} async-done(((bf16[64,8320]{1,0:T(8,128)(2,1)}), bf16[512,8320]{1,0:T(8,128)(2,1)}) %all-gather.3.cloned.1.call-update) | async-done | bytes 8519696 | tf_op jit(solution)/shard_map/all_gather | solution.py:38
  104.5 1.0 convert_reduce_fusion
  105.5 113.1 %all-gather.5.cloned.1.call-done = bf16[1024,8320]{1,0:T(8,128)(2,1)} async-done(((bf16[64,8320]{1,0:T(8,128)(2,1)}), bf16[1024,8320]{1,0:T(8,128)(2,1)}) %all-gather.5.cloned.1.call-update) | async-done | bytes 17039376 | tf_op jit(solution)/shard_map/all_gather | solution.py:39
  218.6 1.4 add_reduce_fusion
  220.0 15.2 %tanh_convert_fusion = bf16[512,1024]{1,0:T(8,128)(2,1)S(1)} fusion(bf16[512,8320]{1,0:T(8,128)(2,1)} %all-gather.3.cloned.1.call-done, bf16[1024,8320]{1,0:T(8,128)(2,1)} %all-gather.5.cloned.1.call-done, f32[512]{0:T(512)S(1)} %convert_reduce_fusion), kind=kOutput, calls=%fused_computation.4 | convolution fusion | flops 8725200896 | bytes 26609664 | tf_op jit(solution)/shard_map/dot_general | solution.py:40
  235.3 0.0 copy-start.2
  235.3 1.8 fusion.1
  237.0 0.0 reduce-scatter.2.cloned.1.call-update
  237.1 0.6 dynamic-slice
  238.3 1.3 add_reduce_fusion.1
  239.6 0.9 multiply_reduce_fusion
  240.5 34.6 %all-reduce = f32[1024]{0:T(1024)S(1)} all-reduce(f32[1024]{0:T(1024)S(1)} %multiply_reduce_fusion), channel_id=3, replica_groups=mesh['blk'=8,'dp'=16] {'dp'}, use_global_device_ids=true, to_apply=%region_2.3.clone | all-reduce | flops 1024 | bytes 8192
  275.0 0.6 dynamic-slice.1
  (9 shorter events, 0.0 us)
Async XLA Ops:
  7.2 4.0 %copy-start.1 = (s32[64]{0:T(128)S(1)}, s32[64]{0:T(128)}, u32[]{:S(2)}) copy-start(s32[64]{0:T(128)} %param.9) | copy-start | bytes 772
  7.2 4.1 %copy-start = (bf16[64,8192]{1,0:T(8,128)(2,1)S(1)}, bf16[64,8192]{1,0:T(8,128)(2,1)}, u32[]{:S(2)}) copy-start(bf16[64,8192]{1,0:T(8,128)(2,1)} %param.8) | copy-start | bytes 3145732
  7.2 97.3 %all-gather.3.cloned.1.call-start = ((), (), s32[]{:S(2)}) async-start(), calls=%async_computation.1 | async-start | bytes 9584640 | tf_op jit(solution)/shard_map/all_gather | solution.py:38
  11.1 207.5 %all-gather.5.cloned.1.call-start = ((), (), s32[]{:S(2)}) async-start(), calls=%async_computation.2 | async-start | bytes 18104320 | tf_op jit(solution)/shard_map/all_gather | solution.py:39
  12.4 263.2 %reduce-scatter.2.cloned.1.call-start = ((), (), s32[]{:S(2)}) async-start(), calls=%async_computation.3 | async-start | bytes 1179648 | tf_op jit(solution)/shard_map/reduce_scatter | solution.py:52
  235.3 1.8 copy-start.2
Sparse Core Ops, SparseCore 0:
  11.2 93.2 all-gather.2
  107.0 111.5 all-gather.4
  237.2 34.5 reduce-scatter.1
where the time goes:
time: 282 us
  waiting for transfers between devices  205 us (73%)
  blocking collectives  34.6 us (12%)
  matrix products  17.9 us (6%)
  between operations  14.5 us (5%)
  other arithmetic  8.7 us (3%)
    all_gather x1, waiting for transfers between devices, local(): te_all = lax.all_gather(te, 'dp', axis=0, tiled=True)  113 us
    all_gather x1, waiting for transfers between devices, local(): tr_all = lax.all_gather(tr, 'blk', axis=0, tiled=True)  92.1 us
    unnamed x1, blocking collectives  34.6 us
    dot_general x1, matrix products, local(): lax.dot_general(tr_all, te_all, (((1,), (1,)), ((), ())), preferred_eleme...  15.2 us
  transfers between devices with their start and end apart: 3, of which 2 were waited for; matrix products, arithmetic and copies ran while one was open for 2% of the time, Pallas kernels for 0%

commit v1 on v0

--- a/solution.py
+++ b/solution.py
@@ -35,7 +35,9 @@
     k = train_grads.shape[1]
     tr = with_side(train_grads, (train_scale,) + split_class(train_class), 0)
     te = with_side(test_grads, split_class(test_class), 4)
-    tr_all = lax.all_gather(tr, "blk", axis=0, tiled=True)
+    tr_all = jnp.concatenate(
+        lax.all_to_all(jnp.stack([tr] * lax.axis_size("blk")), "blk", 0, 0), axis=0
+    )
     te_all = lax.all_gather(te, "dp", axis=0, tiled=True)
     raw = lax.dot_general(
         tr_all, te_all, (((1,), (1,)), ((), ())), preferred_element_type=jnp.float32

time: 282 us -> 264 us (0.936)
  waiting for transfers between devices: 205 us -> 74.4 us
  blocking collectives: 34.6 us -> 145 us
  local copies, waits for them, and re-layouts: 1.19 us -> 5.51 us
    all_to_all x0 -> x1, blocking collectives: none -> 110 us  [local(): lax.all_to_all(jnp.stack([tr] * lax.axis_size('blk')), 'blk', 0, 0)]
    all_gather x1 -> x0, waiting for transfers between devices: 92.1 us -> none  [local(): tr_all = lax.all_gather(tr, 'blk', axis=0, tiled=True)]
    all_gather x1, waiting for transfers between devices: 113 us -> 74.4 us  [local(): te_all = lax.all_gather(te, 'dp', axis=0, tiled=True)]
    unnamed x8 -> x12, local copies, waits for them, and re-layouts: 1.19 us -> 4.48 us
  transfers between devices with their start and end apart: 3 -> 2, of which waited for: 2 -> 1; matrix products, arithmetic and copies ran while one was open for 2% -> 2% of each run, Pallas kernels for 0% -> 0%
where the time goes in v1:
time: 264 us; the launch traced here: 263 us
  blocking collectives  145 us (55%)
  waiting for transfers between devices  74.4 us (28%)
  matrix products  17.9 us (7%)
  between operations  14.8 us (6%)
  other arithmetic  6.17 us (2%)
  local copies, waits for them, and re-layouts  5.51 us (2%)
    all_to_all x1, blocking collectives, local(): lax.all_to_all(jnp.stack([tr] * lax.axis_size('blk')), 'blk', 0, 0)  110 us
    all_gather x1, waiting for transfers between devices, local(): te_all = lax.all_gather(te, 'dp', axis=0, tiled=True)  74.4 us
    unnamed x1, blocking collectives  34.5 us
    dot_general x1, matrix products, local(): lax.dot_general(tr_all, te_all, (((1,), (1,)), ((), ())), preferred_eleme...  15.2 us
  transfers between devices with their start and end apart: 2, of which 1 were waited for; matrix products, arithmetic and copies ran while one was open for 2% of the time, Pallas kernels for 0%

profile of v1, /device:TPU:6, one launch (start us, length us, event | category | flops | bytes accessed | tf_op | source)
XLA Modules:
  0.0 263.5 jit_solution(4431235239110734027)
XLA Ops:
  7.2 0.0 copy-start.3
  7.2 0.0 all-gather.2.cloned.1.call-start
  7.3 0.7 fusion.5
  8.0 0.1 select_select_fusion
  8.1 2.3 pad_maximum_fusion.1
  10.4 0.0 all-gather.2.cloned.1.call-update
  10.5 0.0 reduce-scatter.2.cloned.1.call-start
  10.6 0.1 select_select_fusion.1
  10.7 0.1 pad_maximum_fusion
  10.8 1.0 stack.2
  11.8 110.1 %all_to_all.5 = bf16[8,64,8320]{2,1,0:T(8,128)(2,1)S(1)} all-to-all(bf16[8,64,8320]{2,1,0:T(8,128)(2,1)S(1)} %stack.2), channel_id=1, replica_groups=mesh['blk'=8,'dp'=16] {'blk'}, dimensions={0} | all-to-all | bytes 17039360 | tf_op jit(solution)/shard_map/all_to_all | solution.py:39
  121.9 3.3 %copy-done = bf16[8,64,8320]{2,1,0:T(8,128)(2,1)} copy-done((bf16[8,64,8320]{2,1,0:T(8,128)(2,1)}, bf16[8,64,8320]{2,1,0:T(8,128)(2,1)S(1)}, u32[]{:S(2)}) %copy-start) | copy-done | bytes 8519704
  125.2 0.1 convert_reduce_fusion
  125.3 74.4 %all-gather.2.cloned.1.call-done = bf16[1024,8320]{1,0:T(8,128)(2,1)} async-done(((bf16[64,8320]{1,0:T(8,128)(2,1)}), bf16[1024,8320]{1,0:T(8,128)(2,1)}) %all-gather.2.cloned.1.call-update) | async-done | bytes 17039376 | tf_op jit(solution)/shard_map/all_gather | solution.py:41
  199.6 1.4 add_reduce_fusion
  201.1 15.2 %tanh_convert_fusion = bf16[512,1024]{1,0:T(8,128)(2,1)S(1)} fusion(bf16[512,8320]{1,0:T(8,128)(2,1)} %bitcast.7, bf16[1024,8320]{1,0:T(8,128)(2,1)} %all-gather.2.cloned.1.call-done, f32[512]{0:T(512)S(1)} %convert_reduce_fusion), kind=kOutput, calls=%fused_computation.4 | convolution fusion | flops 8725200896 | bytes 26609664 | tf_op jit(solution)/shard_map/dot_general | solution.py:42
  216.3 0.0 copy-start.4
  216.3 1.8 fusion.1
  218.1 0.0 reduce-scatter.2.cloned.1.call-update
  218.1 0.6 dynamic-slice
  219.4 1.3 add_reduce_fusion.1
  220.6 0.9 multiply_reduce_fusion
  221.5 34.5 %all-reduce = f32[1024]{0:T(1024)S(1)} all-reduce(f32[1024]{0:T(1024)S(1)} %multiply_reduce_fusion), channel_id=3, replica_groups=mesh['blk'=8,'dp'=16] {'dp'}, use_global_device_ids=true, to_apply=%region_2.3.clone | all-reduce | flops 1024 | bytes 8192
  256.1 0.6 dynamic-slice.1
  (12 shorter events, 0.0 us)
Async XLA Ops:
  7.2 3.4 %copy-start.3 = (s32[64]{0:T(128)S(1)}, s32[64]{0:T(128)}, u32[]{:S(2)}) copy-start(s32[64]{0:T(128)} %param.7) | copy-start | bytes 772
  7.2 3.4 %copy-start.2 = (bf16[64]{0:T(256)(128)(2,1)S(1)}, bf16[64]{0:T(256)(128)(2,1)}, u32[]{:S(2)}) copy-start(bf16[64]{0:T(256)(128)(2,1)} %param.6) | copy-start | bytes 388
  7.2 3.5 %copy-start.1 = (bf16[64,8192]{1,0:T(8,128)(2,1)S(1)}, bf16[64,8192]{1,0:T(8,128)(2,1)}, u32[]{:S(2)}) copy-start(bf16[64,8192]{1,0:T(8,128)(2,1)} %param.5) | copy-start | bytes 3145732
  7.2 192.4 %all-gather.2.cloned.1.call-start = ((), (), s32[]{:S(2)}) async-start(), calls=%async_computation.2 | async-start | bytes 18104320 | tf_op jit(solution)/shard_map/all_gather | solution.py:41
  10.5 246.2 %reduce-scatter.2.cloned.1.call-start = ((), (), s32[]{:S(2)}) async-start(), calls=%async_computation.3 | async-start | bytes 1179648 | tf_op jit(solution)/shard_map/reduce_scatter | solution.py:54
  121.9 3.3 %copy-start = (bf16[8,64,8320]{2,1,0:T(8,128)(2,1)}, bf16[8,64,8320]{2,1,0:T(8,128)(2,1)S(1)}, u32[]{:S(2)}) copy-start(bf16[8,64,8320]{2,1,0:T(8,128)(2,1)S(1)} %all_to_all.5) | copy-start | bytes 25559044
  216.3 1.8 copy-start.4
Sparse Core Ops, SparseCore 0:
  10.6 189.0 all-gather.1
  218.2 34.6 reduce-scatter.1
